TPU v7x, 256 devices: a whole 4x4x8 slice. The times are simulated.
256 devices in a mesh: dp: 32 (over z_lo, y, x), tensor: 8 (over z_hi, core).
Axes of the slice: x: 4, y: 4, z: 8 (z_hi: 4, z_lo: 2; z = z_hi * 2 + z_lo), core: 2. Of those that a mesh axis runs over, the one named last changes fastest.
Arguments:
- embeds: bfloat16 [512, 4608], P('dp'), may hold values from -6 to 6
- owner: int32 [64, 8], P('dp'), may hold values from 0 to 7, each once within a row
- pairs: int32 [64, 56, 2], P('dp'), may hold values from 0 to 7, as said below
- pref_weight: bfloat16 [2, 4608, 4608], P(None, 'dp', 'tensor'), may hold values from -0.0625 to 0.0625
- pref_bias: float32 [4608], P('tensor'), may hold values from -3 to 3
- pref_out: float32 [4608], P('tensor'), may hold values from -0.375 to 0.375
- logratio: float32 [512], P('dp'), may hold values from -3 to 3
- attn_out: bfloat16 [32768, 4096], P('dp', 'tensor'), may hold values from -6 to 6
- grad_out: bfloat16 [32768, 4608], P('dp', 'tensor'), may hold values from -6 to 6
- w_out: bfloat16 [4608, 4096], P('dp', 'tensor'), may hold values from -0.09375 to 0.09375
Outputs:
- d_attn: bfloat16 [32768, 4096], P('dp', 'tensor')
- o_grad: float32 [4608, 4096], P('dp', 'tensor')
Inputs may be any that keep to these rules, and one draw needn't show every extreme that they name: `pairs`: the two numbers of a pair differ. Each row of owner names every number once.
All inputs are finite; a program needn't handle non-finite values.
Results may differ from a plain program's by a relative error of at most 0.0049.
Values may be sent and summed in bfloat16 or wider, within the bound.
No kernel may reach another device: no remote copies, remote signals or barrier semaphores. Data moves between devices by JAX's collectives and lax.ppermute only.
A program may use at most 128 MiB of HBM per device.

v0:
```python
import jax
import jax.numpy as jnp
from jax import lax
from jax.sharding import Mesh
from jax.sharding import PartitionSpec as P

eta_scale = 2.0
DP = ("zl", "y", "x")
TP = ("zh", "c")
PLANE = ("y", "x")


def shards(
    embeds, owner, pairs, pref_weight, pref_bias, pref_out, logratio, attn_out, grad_out, w_out
):
    resp_dev = embeds.shape[0]
    prompts_dev = owner.shape[0]
    groups = owner.shape[1]
    npairs = pairs.shape[1]
    width_local = pref_weight.shape[2]
    rows_w = pref_weight.shape[1]
    n_dp = lax.axis_size(DP)
    n_zl = lax.axis_size("zl")
    n_plane = lax.axis_size(PLANE)
    zl = lax.axis_index("zl")
    swap = [(k, (k + 1) % n_zl) for k in range(n_zl)]
    features = lax.all_gather(grad_out, TP, axis=1, tiled=True)
    w_other = lax.ppermute(w_out, "zl", swap)
    other = lax.ppermute(pref_weight, "zl", swap)
    w_pair = jnp.where(zl == 0, jnp.stack([w_out, w_other]), jnp.stack([w_other, w_out]))
    copies = jnp.broadcast_to(w_pair[None], (n_plane,) + w_pair.shape)
    piece = lax.all_to_all(copies, PLANE, 0, 0, tiled=True)
    piece = piece.transpose(1, 0, 2, 3).reshape(-1, w_out.shape[1])
    pair_w = jnp.where(
        zl == 0,
        jnp.concatenate([pref_weight, other], axis=1),
        jnp.concatenate([other, pref_weight], axis=1),
    )
    cols = embeds.reshape(resp_dev, n_zl, n_plane, rows_w).transpose(2, 0, 1, 3)
    cols = cols.reshape(n_plane, resp_dev * n_zl * rows_w // 128, 128)
    cols = lax.all_to_all(cols, PLANE, 0, 0, tiled=True).reshape(n_plane * resp_dev, n_zl * rows_w)
    part = jnp.concatenate(
        [
            jnp.dot(cols, pair_w[0], preferred_element_type=jnp.float32),
            jnp.dot(cols, pair_w[1], preferred_element_type=jnp.float32),
        ],
        axis=1,
    )
    part = part.reshape(n_plane, resp_dev, part.shape[1])
    proj = jnp.sum(lax.all_to_all(part, PLANE, 0, 0, tiled=True), axis=0)
    base = (jnp.arange(prompts_dev, dtype=jnp.int32) * groups)[:, None]
    row_a = base + jnp.take_along_axis(owner, pairs[:, :, 0], axis=1)
    row_b = base + jnp.take_along_axis(owner, pairs[:, :, 1], axis=1)
    upper = proj[:, :width_local][row_a.reshape(-1)]
    lower = proj[:, width_local:][row_b.reshape(-1)]
    pre = (upper + lower).reshape(prompts_dev, npairs, width_local)
    hidden = jax.nn.gelu(pre + pref_bias)
    partial_logit = jnp.sum(hidden * pref_out, axis=-1)
    logit = lax.psum(partial_logit, TP)
    prob = jax.nn.sigmoid(logit)
    numbers = jnp.arange(groups, dtype=jnp.int32)
    first = (pairs[:, :, 0][:, :, None] == numbers).astype(jnp.float32)
    second = (pairs[:, :, 1][:, :, None] == numbers).astype(jnp.float32)
    wins = jnp.sum(prob[:, :, None] * first + (1.0 - prob)[:, :, None] * second, axis=1)
    count = jnp.sum(first + second, axis=1)
    winrate = (wins + 1.0) / (count + 2.0)
    placed = (owner[:, :, None] == numbers).astype(jnp.float32)
    rowrate = jnp.sum(winrate[:, :, None] * placed, axis=1).reshape(-1)
    coef = 2.0 * (logratio - eta_scale * (rowrate - 0.5))
    weighted = (
        (
            features.astype(jnp.float32).reshape(resp_dev, -1, features.shape[1])
            * coef[:, None, None]
        )
        .reshape(features.shape)
        .astype(jnp.bfloat16)
    )
    total_resp = resp_dev * n_dp
    full = lax.dot_general(
        weighted, attn_out, (((0,), (0,)), ((), ())), preferred_element_type=jnp.float32
    )
    full = full.astype(jnp.bfloat16).reshape(n_zl, n_plane, -1, full.shape[1])
    first_half = jnp.where(zl == 0, full[1], full[0])
    own_half = jnp.where(zl == 0, full[0], full[1])
    theirs = jnp.sum(
        lax.all_to_all(first_half, PLANE, 0, 0, tiled=True).astype(jnp.float32), axis=0
    )
    got = lax.ppermute(theirs, "zl", swap)
    shares = lax.all_to_all(own_half, PLANE, 0, 0, tiled=True)
    d_attn = jnp.dot(weighted, piece, preferred_element_type=jnp.float32).astype(jnp.bfloat16)
    shares, d_attn = lax.optimization_barrier((shares, d_attn))
    mine = jnp.sum(shares.astype(jnp.float32), axis=0)
    o_grad = (mine + got) / total_resp
    return (d_attn, o_grad)


def solution(mesh):
    n_zl = 2
    fine = Mesh(
        mesh.devices.reshape(n_zl, mesh.shape["dp"] // (n_zl * 4), 4, mesh.shape["tensor"] // 2, 2),
        ("zl", "y", "x", "zh", "c"),
    )
    return jax.shard_map(
        shards,
        mesh=fine,
        in_specs=(
            P(DP, None),
            P(DP, None),
            P(DP, None, None),
            P(None, DP, TP),
            P(TP),
            P(TP),
            P(DP),
            P(DP, TP),
            P(DP, TP),
            P(DP, TP),
        ),
        out_specs=(P(DP, TP), P(DP, TP)),
        check_vma=False,
    )
```

profile of v0, /device:TPU:64, one launch (start us, length us, event | category | flops | bytes accessed | tf_op | source)
XLA Modules:
  0.0 200.9 jit_solution(1344475992000351544)
XLA Ops:
  7.2 0.7 all-gather.2.cloned.1.call-update
  7.9 2.0 collective-permute-start
  9.9 1.3 reshape.160
  11.2 0.2 copy.21
  11.5 1.1 reshape.161
  12.6 7.0 %all-to-all-start = ((bf16[16,36,128]{2,1,0:T(8,128)(2,1)}), bf16[16,36,128]{2,1,0:T(8,128)(2,1)S(1)}, u32[]{:S(2)}, u32[]{:S(2)}) async-start(bf16[16,36,128]{2,1,0:T(8,128)(2,1)} %reshape.161), calls=%async_computation | async-start | bytes 327680 | tf_op jit(solution)/shard_map/all_to_all | solution.py:41
  19.6 0.2 collective-permute-start.1
  19.8 0.8 fusion.18
  20.6 7.2 %all-to-all-done = bf16[16,36,128]{2,1,0:T(8,128)(2,1)S(1)} async-done(((bf16[16,36,128]{2,1,0:T(8,128)(2,1)}), bf16[16,36,128]{2,1,0:T(8,128)(2,1)S(1)}, u32[]{:S(2)}, u32[]{:S(2)}) %all-to-all-start) | async-done | bytes 147488 | tf_op jit(solution)/shard_map/all_to_all | solution.py:41
  27.8 0.3 reshape.162
  28.1 1.3 maximum_select_fusion
  29.4 0.4 convolution_bitcast_fusion
  29.8 0.4 convolution_bitcast_fusion.1
  30.2 1.4 copy.18
  31.6 3.7 %all-to-all-start.1 = ((f32[16,16,1152]{2,1,0:T(8,128)}), f32[16,16,1152]{2,1,0:T(8,128)S(1)}, u32[]{:S(2)}, u32[]{:S(2)}) async-start(f32[16,16,1152]{2,1,0:T(8,128)} %bitcast.6), calls=%async_computation.1 | async-start | bytes 2359296 | tf_op jit(solution)/shard_map/all_to_all | solution.py:50
  35.3 0.1 reshape.207
  35.4 2.0 %gather_fusion.2 = s32[112]{0:T(128)S(1)} fusion(s32[2,8]{1,0:T(2,128)S(1)} %copy-done.1, s32[112]{0:T(128)S(1)} %reshape.207), kind=kCustom, calls=%fused_computation.clone | custom fusion | bytes 1792 | tf_op jit(solution)/shard_map/jit(take_along_axis)/gather | solution.py:52
  37.4 0.1 reshape.210
  37.5 0.1 reshape.212
  37.6 2.0 %gather_fusion.3 = s32[112]{0:T(128)S(1)} fusion(s32[2,8]{1,0:T(2,128)S(1)} %copy-done.1, s32[112]{0:T(128)S(1)} %reshape.212), kind=kCustom, calls=%fused_computation.1.clone | custom fusion | bytes 1792 | tf_op jit(solution)/shard_map/jit(take_along_axis)/gather | solution.py:53
  39.6 0.1 reshape.215
  39.8 0.1 reshape.165
  39.9 0.1 reshape.164
  40.0 13.0 %all-to-all-done.1 = f32[16,16,1152]{2,1,0:T(8,128)S(1)} async-done(((f32[16,16,1152]{2,1,0:T(8,128)}), f32[16,16,1152]{2,1,0:T(8,128)S(1)}, u32[]{:S(2)}, u32[]{:S(2)}) %all-to-all-start.1) | async-done | bytes 1179680 | tf_op jit(solution)/shard_map/all_to_all | solution.py:50
  53.0 2.6 %broadcast_in_dim.4 = bf16[16,2,144,512]{3,2,1,0:T(8,128)(2,1)} broadcast(bf16[2,144,512]{2,1,0:T(8,128)(2,1)S(1)} %maximum_select_fusion.1), dimensions={1,2,3} | broadcast | bytes 5013504 | tf_op jit(solution)/shard_map/broadcast_in_dim | solution.py:31
  55.7 4.6 %all-to-all-start.3 = ((bf16[16,2,144,512]{3,2,1,0:T(8,128)(2,1)}), bf16[16,2,144,512]{3,2,1,0:T(8,128)(2,1)}, u32[]{:S(2)}, u32[]{:S(2)}) async-start(bf16[16,2,144,512]{3,2,1,0:T(8,128)(2,1)} %broadcast_in_dim.4), calls=%async_computation.3 | async-start | bytes 9437184 | tf_op jit(solution)/shard_map/all_to_all | solution.py:32
  60.4 0.8 gather_fusion.1
  61.2 0.8 gather_fusion
  62.0 0.2 fusion.12
  62.3 0.1 reduce_sum.67
  62.3 16.0 %psum.7 = f32[2,56]{1,0:T(2,128)S(1)} all-reduce(f32[2,56]{1,0:T(2,128)S(1)} %reduce_sum.67), channel_id=1, replica_groups=mesh['zl'=2,'y'=4,'x'=4,'zh'=4,'c'=2] {'zh','c'}, use_global_device_ids=true, to_apply=%region_2.4 | all-reduce | flops 112 | bytes 896 | tf_op jit(solution)/shard_map/psum | solution.py:59
  78.3 0.1 add_reduce_fusion.1
  78.4 0.1 select_reduce_fusion
  78.5 0.1 mul.106
  78.8 29.8 %all-gather.2.cloned.1.call-done = bf16[1024,4608]{0,1:T(8,128)(2,1)} async-done(((bf16[1024,576]{0,1:T(8,128)(2,1)}), bf16[1024,4608]{0,1:T(8,128)(2,1)}) %all-gather.2.cloned.1.call-update) | async-done | bytes 9437200 | tf_op jit(solution)/shard_map/all_gather | solution.py:27
  108.6 9.0 %fusion.2 = bf16[4608,512]{1,0:T(8,128)(2,1)S(1)} fusion(bf16[1024,512]{1,0:T(8,128)(2,1)S(1)} %copy-done, bf16[1024,4608]{0,1:T(8,128)(2,1)} %all-gather.2.cloned.1.call-done, f32[1024]{0:T(1024)S(1)} %mul.109), kind=kOutput, calls=%fused_computation.7 | convolution fusion | flops 4848353280 | bytes 15208448 | tf_op jit(solution)/shard_map/dot_general | solution.py:79
  117.6 1.7 broadcast_select_fusion
  119.3 6.6 %all-to-all-done.3 = bf16[16,2,144,512]{3,2,1,0:T(8,128)(2,1)} async-done(((bf16[16,2,144,512]{3,2,1,0:T(8,128)(2,1)}), bf16[16,2,144,512]{3,2,1,0:T(8,128)(2,1)}, u32[]{:S(2)}, u32[]{:S(2)}) %all-to-all-start.3) | async-done | bytes 4718624 | tf_op jit(solution)/shard_map/all_to_all | solution.py:32
  125.9 32.7 %all_to_all.25 = bf16[16,144,512]{2,1,0:T(8,128)(2,1)} all-to-all(bf16[16,144,512]{2,1,0:T(8,128)(2,1)S(1)} %bitcast.40), channel_id=1, replica_groups=mesh['zl'=2,'y'=4,'x'=4,'zh'=4,'c'=2] {'y','x'}, dimensions={0} | all-to-all | bytes 4718592 | tf_op jit(solution)/shard_map/all_to_all | solution.py:86
  158.6 3.7 %all-to-all-start.2 = ((bf16[16,144,512]{2,1,0:T(8,128)(2,1)}), bf16[16,144,512]{2,1,0:T(8,128)(2,1)S(1)}, u32[]{:S(2)}, u32[]{:S(2)}) async-start(bf16[16,144,512]{2,1,0:T(8,128)(2,1)} %bitcast.39), calls=%async_computation.2 | async-start | bytes 4718592 | tf_op jit(solution)/shard_map/all_to_all | solution.py:89
  162.4 2.8 %copy.19 = bf16[16,2,144,512]{3,2,0,1:T(8,128)(2,1)S(1)} copy(bf16[16,2,144,512]{3,2,1,0:T(8,128)(2,1)} %all-to-all-done.3) | data formatting | bytes 9437184 | tf_op jit(solution)/shard_map/all_to_all | solution.py:32
  165.2 0.3 copy-done.2
  165.5 1.0 convert_reduce_fusion
  166.5 0.3 collective-permute-start.2
  166.8 8.8 %fusion.3 = bf16[1024,512]{1,0:T(8,128)(2,1)} fusion(bf16[4608,512]{1,0:T(8,128)(2,1)S(1)} %bitcast.41, bf16[1024,4608]{0,1:T(8,128)(2,1)} %all-gather.2.cloned.1.call-done, f32[1024]{0:T(1024)S(1)} %mul.109), kind=kOutput, calls=%fused_computation.12 | convolution fusion | flops 4846518272 | bytes 15208448 | tf_op jit(solution)/shard_map/dot_general | solution.py:90
  175.6 16.3 %all-to-all-done.2 = bf16[16,144,512]{2,1,0:T(8,128)(2,1)S(1)} async-done(((bf16[16,144,512]{2,1,0:T(8,128)(2,1)}), bf16[16,144,512]{2,1,0:T(8,128)(2,1)S(1)}, u32[]{:S(2)}, u32[]{:S(2)}) %all-to-all-start.2) | async-done | bytes 2359328 | tf_op jit(solution)/shard_map/all_to_all | solution.py:89
  192.0 0.3 convert_reduce_fusion.1
  192.3 1.7 add_multiply_fusion
  (35 shorter events, 0.6 us)
Async XLA Ops:
  7.2 101.4 %copy-start = (bf16[1024,512]{1,0:T(8,128)(2,1)S(1)}, bf16[1024,512]{1,0:T(8,128)(2,1)}, u32[]{:S(2)}) copy-start(bf16[1024,512]{1,0:T(8,128)(2,1)} %param.19) | copy-start | bytes 3145732
  7.2 101.4 %all-gather.2.cloned.1.call-start = ((), (), s32[]{:S(2)}) async-start(), calls=%async_computation.5 | async-start | bytes 10616832 | tf_op jit(solution)/shard_map/all_gather | solution.py:27
  7.9 20.2 %collective-permute-start = (bf16[2,144,576]{2,1,0:T(8,128)(2,1)}, bf16[2,144,576]{2,1,0:T(8,128)(2,1)S(1)}, u32[]{:S(2)}, u32[]{:S(2)}) collective-permute-start(bf16[2,144,576]{2,1,0:T(8,128)(2,1)} %param.15), channel_id=1, source_target_pairs={{0,128},{128,0},{1,129},{129,1},{2,130},{130,2},{3,131},{131,3},{4... | collective-permute-start | bytes 995336 | tf_op jit(solution)/shard_map/ppermute | solution.py:29
  12.6 15.2 %all-to-all-start = ((bf16[16,36,128]{2,1,0:T(8,128)(2,1)}), bf16[16,36,128]{2,1,0:T(8,128)(2,1)S(1)}, u32[]{:S(2)}, u32[]{:S(2)}) async-start(bf16[16,36,128]{2,1,0:T(8,128)(2,1)} %reshape.161), calls=%async_computation | async-start | bytes 327680 | tf_op jit(solution)/shard_map/all_to_all | solution.py:41
  19.6 20.3 %collective-permute-start.1 = (bf16[144,512]{1,0:T(8,128)(2,1)}, bf16[144,512]{1,0:T(8,128)(2,1)S(1)}, u32[]{:S(2)}, u32[]{:S(2)}) collective-permute-start(bf16[144,512]{1,0:T(8,128)(2,1)} %param.21), channel_id=1, source_target_pairs={{0,128},{128,0},{1,129},{129,1},{2,130},{130,2},{3,131},{131,3},{4... | collective-permute-start | bytes 442376 | tf_op jit(solution)/shard_map/ppermute | solution.py:28
  29.4 6.0 %copy-start.1 = (s32[2,8]{1,0:T(2,128)S(1)}, s32[2,8]{1,0:T(2,128)}, u32[]{:S(2)}) copy-start(s32[2,8]{1,0:T(2,128)} %param.13) | copy-start | bytes 196
  30.1 9.8 %copy-start.3 = (bf16[144,512]{1,0:T(8,128)(2,1)S(1)}, bf16[144,512]{1,0:T(8,128)(2,1)}, u32[]{:S(2)}) copy-start(bf16[144,512]{1,0:T(8,128)(2,1)} %param.21) | copy-start | bytes 442372
  31.6 21.4 %all-to-all-start.1 = ((f32[16,16,1152]{2,1,0:T(8,128)}), f32[16,16,1152]{2,1,0:T(8,128)S(1)}, u32[]{:S(2)}, u32[]{:S(2)}) async-start(f32[16,16,1152]{2,1,0:T(8,128)} %bitcast.6), calls=%async_computation.1 | async-start | bytes 2359296 | tf_op jit(solution)/shard_map/all_to_all | solution.py:50
  55.7 70.3 %all-to-all-start.3 = ((bf16[16,2,144,512]{3,2,1,0:T(8,128)(2,1)}), bf16[16,2,144,512]{3,2,1,0:T(8,128)(2,1)}, u32[]{:S(2)}, u32[]{:S(2)}) async-start(bf16[16,2,144,512]{3,2,1,0:T(8,128)(2,1)} %broadcast_in_dim.4), calls=%async_computation.3 | async-start | bytes 9437184 | tf_op jit(solution)/shard_map/all_to_all | solution.py:32
  60.2 1.8 copy-start.4
  60.2 1.8 copy-start.5
  60.2 18.4 %copy-start.6 = (f32[16]{0:T(128)S(1)}, f32[16]{0:T(128)}, u32[]{:S(2)}) copy-start(f32[16]{0:T(128)} %param.18) | copy-start | bytes 196
  158.6 33.3 %all-to-all-start.2 = ((bf16[16,144,512]{2,1,0:T(8,128)(2,1)}), bf16[16,144,512]{2,1,0:T(8,128)(2,1)S(1)}, u32[]{:S(2)}, u32[]{:S(2)}) async-start(bf16[16,144,512]{2,1,0:T(8,128)(2,1)} %bitcast.39), calls=%async_computation.2 | async-start | bytes 4718592 | tf_op jit(solution)/shard_map/all_to_all | solution.py:89
  162.4 3.1 %copy-start.2 = (bf16[16,144,512]{2,1,0:T(8,128)(2,1)S(1)}, bf16[16,144,512]{2,1,0:T(8,128)(2,1)}, u32[]{:S(2)}) copy-start(bf16[16,144,512]{2,1,0:T(8,128)(2,1)} %all_to_all.25) | copy-start | bytes 7077892
  166.5 25.8 %collective-permute-start.2 = (f32[144,512]{1,0:T(8,128)}, f32[144,512]{1,0:T(8,128)}, u32[]{:S(2)}, u32[]{:S(2)}) collective-permute-start(f32[144,512]{1,0:T(8,128)} %convert_reduce_fusion), channel_id=1, source_target_pairs={{0,128},{128,0},{1,129},{129,1},{2,130},{130,2},{3,131},{131,3},{4... | collective-permute-start | bytes 884744 | tf_op jit(solution)/shard_map/ppermute | solution.py:88
Sparse Core Ops, SparseCore 0:
  9.8 98.6 all-gather.1
where the time goes:
time: 201 us
  waiting for transfers between devices  73.7 us (37%)
  blocking collectives  48.7 us (24%)
  starting transfers between devices  21.5 us (11%)
  matrix products  18.6 us (9%)
  local copies, waits for them, and re-layouts  17.3 us (9%)
  between operations  14.3 us (7%)
  other arithmetic  6.84 us (3%)
    all_to_all x1, blocking collectives, shards(): lax.all_to_all(first_half, PLANE, 0, 0, tiled=True).astype(jnp.float32)  32.7 us
    all_gather x1, waiting for transfers between devices, shards(): features = lax.all_gather(grad_out, TP, axis=1, tiled=True)  29.8 us
    all_to_all x1, waiting for transfers between devices, shards(): shares = lax.all_to_all(own_half, PLANE, 0, 0, tiled=True)  16.3 us
    psum x1, blocking collectives, shards(): logit = lax.psum(partial_logit, TP)  16 us
    all_to_all x1, waiting for transfers between devices, shards(): proj = jnp.sum(lax.all_to_all(part, PLANE, 0, 0, tiled=True), axis=0)  13 us
    dot_general x1, matrix products, shards(): lax.dot_general(weighted, attn_out, (((0,), (0,)), ((), ())), preferred_e...  9.03 us
    dot_general x1, matrix products, shards(): jnp.dot(weighted, piece, preferred_element_type=jnp.float32)  8.83 us
    all_to_all x1, waiting for transfers between devices, shards(): lax.all_to_all(cols, PLANE, 0, 0, tiled=True)  7.21 us
  transfers between devices with their start and end apart: 8, of which 5 were waited for; matrix products, arithmetic and copies ran while one was open for 20% of the time, Pallas kernels for 0%

commit v1 on v0

--- a/solution.py
+++ b/solution.py
@@ -56,7 +56,7 @@
     pre = (upper + lower).reshape(prompts_dev, npairs, width_local)
     hidden = jax.nn.gelu(pre + pref_bias)
     partial_logit = jnp.sum(hidden * pref_out, axis=-1)
-    logit = lax.psum(partial_logit, TP)
+    logit = jnp.sum(lax.all_gather(partial_logit, TP), axis=0)
     prob = jax.nn.sigmoid(logit)
     numbers = jnp.arange(groups, dtype=jnp.int32)
     first = (pairs[:, :, 0][:, :, None] == numbers).astype(jnp.float32)

time: 201 us -> 201 us (level)
  blocking collectives: 48.7 us -> 44.8 us
  waiting for transfers between devices: 73.7 us -> 77.4 us
    psum x1 -> x0, blocking collectives: 16 us -> none  [shards(): logit = lax.psum(partial_logit, TP)]
    all_gather x0 -> x1, blocking collectives: none -> 12.1 us  [shards(): logit = jnp.sum(lax.all_gather(partial_logit, TP), axis=0)]
    all_gather x1, waiting for transfers between devices: 29.8 us -> 33.5 us  [shards(): features = lax.all_gather(grad_out, TP, axis=1, tiled=True)]
where the time goes in v1:
time: 201 us
  waiting for transfers between devices  77.4 us (39%)
  blocking collectives  44.8 us (22%)
  starting transfers between devices  21.7 us (11%)
  matrix products  18.6 us (9%)
  local copies, waits for them, and re-layouts  17.3 us (9%)
  between operations  14.3 us (7%)
  other arithmetic  6.86 us (3%)
    all_gather x1, waiting for transfers between devices, shards(): features = lax.all_gather(grad_out, TP, axis=1, tiled=True)  33.5 us
    all_to_all x1, blocking collectives, shards(): lax.all_to_all(first_half, PLANE, 0, 0, tiled=True).astype(jnp.float32)  32.7 us
    all_to_all x1, waiting for transfers between devices, shards(): shares = lax.all_to_all(own_half, PLANE, 0, 0, tiled=True)  16.2 us
    all_to_all x1, waiting for transfers between devices, shards(): proj = jnp.sum(lax.all_to_all(part, PLANE, 0, 0, tiled=True), axis=0)  13 us
    all_gather x1, blocking collectives, shards(): logit = jnp.sum(lax.all_gather(partial_logit, TP), axis=0)  12.1 us
    dot_general x1, matrix products, shards(): lax.dot_general(weighted, attn_out, (((0,), (0,)), ((), ())), preferred_e...  9.03 us
    dot_general x1, matrix products, shards(): jnp.dot(weighted, piece, preferred_element_type=jnp.float32)  8.83 us
    all_to_all x1, waiting for transfers between devices, shards(): lax.all_to_all(cols, PLANE, 0, 0, tiled=True)  7.21 us
  transfers between devices with their start and end apart: 8, of which 5 were waited for; matrix products, arithmetic and copies ran while one was open for 20% of the time, Pallas kernels for 0%

profile of v1, /device:TPU:64, one launch (start us, length us, event | category | flops | bytes accessed | tf_op | source)
XLA Modules:
  0.0 200.9 jit_solution(349256657537173928)
XLA Ops:
  7.2 0.7 all-gather.2.cloned.1.call-update
  7.9 2.0 collective-permute-start
  9.9 1.3 reshape.168
  11.2 0.2 copy.21
  11.5 1.1 reshape.169
  12.6 7.0 %all-to-all-start = ((bf16[16,36,128]{2,1,0:T(8,128)(2,1)}), bf16[16,36,128]{2,1,0:T(8,128)(2,1)S(1)}, u32[]{:S(2)}, u32[]{:S(2)}) async-start(bf16[16,36,128]{2,1,0:T(8,128)(2,1)} %reshape.169), calls=%async_computation | async-start | bytes 327680 | tf_op jit(solution)/shard_map/all_to_all | solution.py:41
  19.6 0.2 collective-permute-start.1
  19.8 0.8 fusion.18
  20.6 7.2 %all-to-all-done = bf16[16,36,128]{2,1,0:T(8,128)(2,1)S(1)} async-done(((bf16[16,36,128]{2,1,0:T(8,128)(2,1)}), bf16[16,36,128]{2,1,0:T(8,128)(2,1)S(1)}, u32[]{:S(2)}, u32[]{:S(2)}) %all-to-all-start) | async-done | bytes 147488 | tf_op jit(solution)/shard_map/all_to_all | solution.py:41
  27.8 0.3 reshape.170
  28.1 1.3 maximum_select_fusion
  29.4 0.4 convolution_bitcast_fusion
  29.8 0.4 convolution_bitcast_fusion.1
  30.2 1.4 copy.18
  31.6 3.7 %all-to-all-start.1 = ((f32[16,16,1152]{2,1,0:T(8,128)}), f32[16,16,1152]{2,1,0:T(8,128)S(1)}, u32[]{:S(2)}, u32[]{:S(2)}) async-start(f32[16,16,1152]{2,1,0:T(8,128)} %bitcast.6), calls=%async_computation.1 | async-start | bytes 2359296 | tf_op jit(solution)/shard_map/all_to_all | solution.py:50
  35.3 0.1 reshape.215
  35.4 2.0 %gather_fusion.2 = s32[112]{0:T(128)S(1)} fusion(s32[2,8]{1,0:T(2,128)S(1)} %copy-done.1, s32[112]{0:T(128)S(1)} %reshape.215), kind=kCustom, calls=%fused_computation.clone | custom fusion | bytes 1792 | tf_op jit(solution)/shard_map/jit(take_along_axis)/gather | solution.py:52
  37.4 0.1 reshape.218
  37.5 0.1 reshape.220
  37.6 2.0 %gather_fusion.3 = s32[112]{0:T(128)S(1)} fusion(s32[2,8]{1,0:T(2,128)S(1)} %copy-done.1, s32[112]{0:T(128)S(1)} %reshape.220), kind=kCustom, calls=%fused_computation.1.clone | custom fusion | bytes 1792 | tf_op jit(solution)/shard_map/jit(take_along_axis)/gather | solution.py:53
  39.6 0.1 reshape.223
  39.8 0.1 reshape.173
  39.9 0.1 reshape.172
  40.0 13.0 %all-to-all-done.1 = f32[16,16,1152]{2,1,0:T(8,128)S(1)} async-done(((f32[16,16,1152]{2,1,0:T(8,128)}), f32[16,16,1152]{2,1,0:T(8,128)S(1)}, u32[]{:S(2)}, u32[]{:S(2)}) %all-to-all-start.1) | async-done | bytes 1179680 | tf_op jit(solution)/shard_map/all_to_all | solution.py:50
  53.0 2.6 %broadcast_in_dim.4 = bf16[16,2,144,512]{3,2,1,0:T(8,128)(2,1)} broadcast(bf16[2,144,512]{2,1,0:T(8,128)(2,1)S(1)} %maximum_select_fusion.1), dimensions={1,2,3} | broadcast | bytes 5013504 | tf_op jit(solution)/shard_map/broadcast_in_dim | solution.py:31
  55.7 4.6 %all-to-all-start.3 = ((bf16[16,2,144,512]{3,2,1,0:T(8,128)(2,1)}), bf16[16,2,144,512]{3,2,1,0:T(8,128)(2,1)}, u32[]{:S(2)}, u32[]{:S(2)}) async-start(bf16[16,2,144,512]{3,2,1,0:T(8,128)(2,1)} %broadcast_in_dim.4), calls=%async_computation.3 | async-start | bytes 9437184 | tf_op jit(solution)/shard_map/all_to_all | solution.py:32
  60.4 0.8 gather_fusion.1
  61.2 0.8 gather_fusion
  62.0 0.2 fusion.12
  62.3 0.1 all_gather.10
  62.3 12.1 %all_gather.11 = f32[8,2,56]{2,1,0:T(2,128)S(1)} all-gather(f32[1,2,56]{2,1,0:T(2,128)S(1)} %all_gather.10), channel_id=1, replica_groups=mesh['zl'=2,'y'=4,'x'=4,'zh'=4,'c'=2] {'zh','c'}, dimensions={0}, use_global_device_ids=true | all-gather | bytes 4032 | tf_op jit(solution)/shard_map/all_gather | solution.py:59
  74.5 0.1 add_reduce_fusion.1
  74.6 0.1 select_reduce_fusion
  74.7 0.1 mul.106
  74.9 33.5 %all-gather.2.cloned.1.call-done = bf16[1024,4608]{0,1:T(8,128)(2,1)} async-done(((bf16[1024,576]{0,1:T(8,128)(2,1)}), bf16[1024,4608]{0,1:T(8,128)(2,1)}) %all-gather.2.cloned.1.call-update) | async-done | bytes 9437200 | tf_op jit(solution)/shard_map/all_gather | solution.py:27
  108.4 9.0 %fusion.2 = bf16[4608,512]{1,0:T(8,128)(2,1)S(1)} fusion(bf16[1024,512]{1,0:T(8,128)(2,1)S(1)} %copy-done, bf16[1024,4608]{0,1:T(8,128)(2,1)} %all-gather.2.cloned.1.call-done, f32[1024]{0:T(1024)S(1)} %mul.109), kind=kOutput, calls=%fused_computation.7 | convolution fusion | flops 4848353280 | bytes 15208448 | tf_op jit(solution)/shard_map/dot_general | solution.py:79
  117.4 1.7 broadcast_select_fusion
  119.1 6.8 %all-to-all-done.3 = bf16[16,2,144,512]{3,2,1,0:T(8,128)(2,1)} async-done(((bf16[16,2,144,512]{3,2,1,0:T(8,128)(2,1)}), bf16[16,2,144,512]{3,2,1,0:T(8,128)(2,1)}, u32[]{:S(2)}, u32[]{:S(2)}) %all-to-all-start.3) | async-done | bytes 4718624 | tf_op jit(solution)/shard_map/all_to_all | solution.py:32
  125.9 32.7 %all_to_all.25 = bf16[16,144,512]{2,1,0:T(8,128)(2,1)} all-to-all(bf16[16,144,512]{2,1,0:T(8,128)(2,1)S(1)} %bitcast.40), channel_id=1, replica_groups=mesh['zl'=2,'y'=4,'x'=4,'zh'=4,'c'=2] {'y','x'}, dimensions={0} | all-to-all | bytes 4718592 | tf_op jit(solution)/shard_map/all_to_all | solution.py:86
  158.6 3.9 %all-to-all-start.2 = ((bf16[16,144,512]{2,1,0:T(8,128)(2,1)}), bf16[16,144,512]{2,1,0:T(8,128)(2,1)S(1)}, u32[]{:S(2)}, u32[]{:S(2)}) async-start(bf16[16,144,512]{2,1,0:T(8,128)(2,1)} %bitcast.39), calls=%async_computation.2 | async-start | bytes 4718592 | tf_op jit(solution)/shard_map/all_to_all | solution.py:89
  162.6 2.8 %copy.19 = bf16[16,2,144,512]{3,2,0,1:T(8,128)(2,1)S(1)} copy(bf16[16,2,144,512]{3,2,1,0:T(8,128)(2,1)} %all-to-all-done.3) | data formatting | bytes 9437184 | tf_op jit(solution)/shard_map/all_to_all | solution.py:32
  165.4 0.3 copy-done.2
  165.6 1.0 convert_reduce_fusion
  166.7 0.3 collective-permute-start.2
  167.0 8.8 %fusion.3 = bf16[1024,512]{1,0:T(8,128)(2,1)} fusion(bf16[4608,512]{1,0:T(8,128)(2,1)S(1)} %bitcast.41, bf16[1024,4608]{0,1:T(8,128)(2,1)} %all-gather.2.cloned.1.call-done, f32[1024]{0:T(1024)S(1)} %mul.109), kind=kOutput, calls=%fused_computation.12 | convolution fusion | flops 4846518272 | bytes 15208448 | tf_op jit(solution)/shard_map/dot_general | solution.py:90
  175.8 16.2 %all-to-all-done.2 = bf16[16,144,512]{2,1,0:T(8,128)(2,1)S(1)} async-done(((bf16[16,144,512]{2,1,0:T(8,128)(2,1)}), bf16[16,144,512]{2,1,0:T(8,128)(2,1)S(1)}, u32[]{:S(2)}, u32[]{:S(2)}) %all-to-all-start.2) | async-done | bytes 2359328 | tf_op jit(solution)/shard_map/all_to_all | solution.py:89
  192.0 0.3 convert_reduce_fusion.1
  192.3 1.7 add_multiply_fusion
  (36 shorter events, 0.6 us)
Async XLA Ops:
  7.2 101.2 %copy-start = (bf16[1024,512]{1,0:T(8,128)(2,1)S(1)}, bf16[1024,512]{1,0:T(8,128)(2,1)}, u32[]{:S(2)}) copy-start(bf16[1024,512]{1,0:T(8,128)(2,1)} %param.19) | copy-start | bytes 3145732
  7.2 101.2 %all-gather.2.cloned.1.call-start = ((), (), s32[]{:S(2)}) async-start(), calls=%async_computation.5 | async-start | bytes 10616832 | tf_op jit(solution)/shard_map/all_gather | solution.py:27
  7.9 20.2 %collective-permute-start = (bf16[2,144,576]{2,1,0:T(8,128)(2,1)}, bf16[2,144,576]{2,1,0:T(8,128)(2,1)S(1)}, u32[]{:S(2)}, u32[]{:S(2)}) collective-permute-start(bf16[2,144,576]{2,1,0:T(8,128)(2,1)} %param.15), channel_id=1, source_target_pairs={{0,128},{128,0},{1,129},{129,1},{2,130},{130,2},{3,131},{131,3},{4... | collective-permute-start | bytes 995336 | tf_op jit(solution)/shard_map/ppermute | solution.py:29
  12.6 15.2 %all-to-all-start = ((bf16[16,36,128]{2,1,0:T(8,128)(2,1)}), bf16[16,36,128]{2,1,0:T(8,128)(2,1)S(1)}, u32[]{:S(2)}, u32[]{:S(2)}) async-start(bf16[16,36,128]{2,1,0:T(8,128)(2,1)} %reshape.169), calls=%async_computation | async-start | bytes 327680 | tf_op jit(solution)/shard_map/all_to_all | solution.py:41
  19.6 20.3 %collective-permute-start.1 = (bf16[144,512]{1,0:T(8,128)(2,1)}, bf16[144,512]{1,0:T(8,128)(2,1)S(1)}, u32[]{:S(2)}, u32[]{:S(2)}) collective-permute-start(bf16[144,512]{1,0:T(8,128)(2,1)} %param.21), channel_id=1, source_target_pairs={{0,128},{128,0},{1,129},{129,1},{2,130},{130,2},{3,131},{131,3},{4... | collective-permute-start | bytes 442376 | tf_op jit(solution)/shard_map/ppermute | solution.py:28
  29.4 6.0 %copy-start.1 = (s32[2,8]{1,0:T(2,128)S(1)}, s32[2,8]{1,0:T(2,128)}, u32[]{:S(2)}) copy-start(s32[2,8]{1,0:T(2,128)} %param.13) | copy-start | bytes 196
  30.1 9.8 %copy-start.3 = (bf16[144,512]{1,0:T(8,128)(2,1)S(1)}, bf16[144,512]{1,0:T(8,128)(2,1)}, u32[]{:S(2)}) copy-start(bf16[144,512]{1,0:T(8,128)(2,1)} %param.21) | copy-start | bytes 442372
  31.6 21.4 %all-to-all-start.1 = ((f32[16,16,1152]{2,1,0:T(8,128)}), f32[16,16,1152]{2,1,0:T(8,128)S(1)}, u32[]{:S(2)}, u32[]{:S(2)}) async-start(f32[16,16,1152]{2,1,0:T(8,128)} %bitcast.6), calls=%async_computation.1 | async-start | bytes 2359296 | tf_op jit(solution)/shard_map/all_to_all | solution.py:50
  55.7 70.3 %all-to-all-start.3 = ((bf16[16,2,144,512]{3,2,1,0:T(8,128)(2,1)}), bf16[16,2,144,512]{3,2,1,0:T(8,128)(2,1)}, u32[]{:S(2)}, u32[]{:S(2)}) async-start(bf16[16,2,144,512]{3,2,1,0:T(8,128)(2,1)} %broadcast_in_dim.4), calls=%async_computation.3 | async-start | bytes 9437184 | tf_op jit(solution)/shard_map/all_to_all | solution.py:32
  60.2 1.8 copy-start.4
  60.2 1.8 copy-start.5
  60.2 14.5 %copy-start.6 = (f32[16]{0:T(128)S(1)}, f32[16]{0:T(128)}, u32[]{:S(2)}) copy-start(f32[16]{0:T(128)} %param.18) | copy-start | bytes 196
  158.6 33.3 %all-to-all-start.2 = ((bf16[16,144,512]{2,1,0:T(8,128)(2,1)}), bf16[16,144,512]{2,1,0:T(8,128)(2,1)S(1)}, u32[]{:S(2)}, u32[]{:S(2)}) async-start(bf16[16,144,512]{2,1,0:T(8,128)(2,1)} %bitcast.39), calls=%async_computation.2 | async-start | bytes 4718592 | tf_op jit(solution)/shard_map/all_to_all | solution.py:89
  162.6 3.1 %copy-start.2 = (bf16[16,144,512]{2,1,0:T(8,128)(2,1)S(1)}, bf16[16,144,512]{2,1,0:T(8,128)(2,1)}, u32[]{:S(2)}) copy-start(bf16[16,144,512]{2,1,0:T(8,128)(2,1)} %all_to_all.25) | copy-start | bytes 7077892
  166.7 25.6 %collective-permute-start.2 = (f32[144,512]{1,0:T(8,128)}, f32[144,512]{1,0:T(8,128)}, u32[]{:S(2)}, u32[]{:S(2)}) collective-permute-start(f32[144,512]{1,0:T(8,128)} %convert_reduce_fusion), channel_id=1, source_target_pairs={{0,128},{128,0},{1,129},{129,1},{2,130},{130,2},{3,131},{131,3},{4... | collective-permute-start | bytes 884744 | tf_op jit(solution)/shard_map/ppermute | solution.py:88
Sparse Core Ops, SparseCore 0:
  9.8 98.4 all-gather.1
